TPU v7x, 32 devices: a whole 2x2x4 slice. The times are simulated.
32 devices in a mesh: band: 8 (over z, core), col: 4 (over y, x).
Axes of the slice: x: 2, y: 2, z: 4, core: 2. Of those that a mesh axis runs over, the one named last changes fastest.
Arguments:
- cells: bfloat16 [32, 256, 768], P('band', 'col'), may hold values from -25 to 25
- summary: bfloat16 [8, 256, 768], P('band', 'col'), may hold values from -6 to 6
- owner: int32 [4], P('col'), may hold values from 0 to 7
- schema: int32 [32, 256], P('band', 'col'), may hold values from 0 to 15
- w_qkv: bfloat16 [768, 2304], replicated, may hold values from -0.21875 to 0.21875
- w_out: bfloat16 [768, 768], replicated, may hold values from -0.625 to 0.625
- gain_attn: float32 [768], replicated, may hold values from 0.5 to 1.5
- w_up: bfloat16 [768, 3072], replicated, may hold values from -0.21875 to 0.21875
- w_down: bfloat16 [3072, 768], replicated, may hold values from -0.109375 to 0.109375
- gain_ffn: float32 [768], replicated, may hold values from 0.5 to 1.5
Outputs:
- cells_out: bfloat16 [32, 256, 768], P('band', 'col')
- summary_out: bfloat16 [256, 768], P('col')
Inputs may be any that keep to these rules, and one draw needn't show every extreme that they name: `owner`: each entry names the band whose summary tokens its column group reads. `schema`: bit g of an entry allows the cell to attend to the row's cells of column group g; the cell's own group is allowed whatever the bits.
All inputs are finite; a program needn't handle non-finite values.
Results may differ from a plain program's by a relative error of at most 0.019.
Values may be sent and summed in bfloat16 or wider, within the bound.
No kernel may reach another device: no remote copies, remote signals or barrier semaphores. Data moves between devices by JAX's collectives and lax.ppermute only.
A program may use at most 128 MiB of HBM per device.

v0:
```python
import jax
import jax.numpy as jnp
from jax import lax
from jax.sharding import PartitionSpec as P

HEADS = 12
HEAD_DIM = 64


def spread_2(value, axis, source):
    kept = jnp.where(lax.axis_index(axis) == source, value, 0).astype(value.dtype)
    return lax.psum(kept, axis)


def layer_norm(values, gain_vec):
    center = values - jnp.mean(values, -1, keepdims=True)
    spread = jnp.mean(center * center, -1, keepdims=True)
    return center * lax.rsqrt(spread + 1e-05) * gain_vec


def finish(tokens_in, attended, w_out, gain_attn, w_up, w_down, gain_ffn):
    mixed_out = jnp.dot(attended, w_out, preferred_element_type=jnp.float32)
    hidden = layer_norm(tokens_in.astype(jnp.float32) + mixed_out, gain_attn).astype(jnp.bfloat16)
    inner_act = jax.nn.gelu(jnp.dot(hidden, w_up, preferred_element_type=jnp.float32)).astype(
        jnp.bfloat16
    )
    outer_out = jnp.dot(inner_act, w_down, preferred_element_type=jnp.float32)
    return layer_norm(hidden.astype(jnp.float32) + outer_out, gain_ffn).astype(jnp.bfloat16)


def project(values, weight):
    return jnp.dot(values, weight, preferred_element_type=jnp.float32).astype(jnp.bfloat16)


def head_sum(values):
    dims = values.shape[:-1]
    return values.reshape(dims + (HEADS, HEAD_DIM)).sum(-1)


def head_spread(values):
    dims = values.shape[:-1]
    return jnp.broadcast_to(values[..., None], dims + (HEADS, HEAD_DIM)).reshape(
        dims + (HEADS * HEAD_DIM,)
    )


def local(cells, summary, owner, schema, w_qkv, w_out, gain_attn, w_up, w_down, gain_ffn):
    row_count, cols_dev, model_width = cells.shape
    own_group = lax.axis_index("col")
    score_scale = HEAD_DIM ** (-0.5)
    flat_cells = cells.reshape(row_count * cols_dev, model_width)
    w_kv = w_qkv[:, model_width:]
    tokens = spread_2(summary[0], "band", owner[0])
    row_cells = lax.all_gather(cells, "col", axis=1, tiled=True)
    width_now = row_cells.shape[1]
    qkv_cells = project(flat_cells, w_qkv).reshape(row_count, cols_dev, 3 * model_width)
    queries = qkv_cells[:, :, :model_width]
    own_keys = qkv_cells[:, :, model_width : 2 * model_width].astype(jnp.float32)
    own_vals = qkv_cells[:, :, 2 * model_width :].astype(jnp.float32)
    summary_qkv = project(tokens, w_qkv)
    sum_queries = summary_qkv[:, :model_width]
    sum_keys = summary_qkv[:, model_width : 2 * model_width]
    sum_vals = summary_qkv[:, 2 * model_width :]
    sq = sum_queries.astype(jnp.float32)
    col_scores = head_sum(sq[None] * own_keys) * score_scale
    self_scores = head_sum(sq * sum_keys.astype(jnp.float32)) * score_scale
    col_top = jnp.maximum(lax.pmax(col_scores.max(0), "band"), self_scores)
    col_exp = jnp.exp(col_scores - col_top[None])
    self_exp = jnp.exp(self_scores - col_top)
    col_weights = head_spread(col_exp.astype(jnp.bfloat16).astype(jnp.float32))
    col_mixed = (col_weights * own_vals).sum(0)
    col_total = col_exp.sum(0)
    packed = jnp.concatenate([col_mixed, col_total], axis=-1)
    packed = lax.psum(packed, "band")
    col_mixed = packed[:, :model_width]
    col_total = packed[:, model_width:] + self_exp
    self_weights = head_spread(self_exp.astype(jnp.bfloat16).astype(jnp.float32))
    col_mixed = col_mixed + self_weights * sum_vals.astype(jnp.float32)
    summary_att = (col_mixed / head_spread(col_total)).astype(jnp.bfloat16)
    row_kv = project(row_cells.reshape(row_count * width_now, model_width), w_kv)
    row_kv = row_kv.reshape(row_count, width_now, 2 * model_width)
    q4 = queries.reshape(row_count, cols_dev, HEADS, HEAD_DIM)
    k4 = row_kv[:, :, :model_width].reshape(row_count, width_now, HEADS, HEAD_DIM)
    v4 = row_kv[:, :, model_width:].reshape(row_count, width_now, HEADS, HEAD_DIM)
    sk = sum_keys.reshape(cols_dev, HEADS, HEAD_DIM)
    sv = sum_vals.reshape(cols_dev, HEADS, HEAD_DIM)
    key_groups = jnp.arange(width_now, dtype=jnp.int32) // cols_dev
    allowed = (jnp.right_shift(schema[:, :, None], key_groups[None, None, :]) & 1 == 1) | (
        key_groups == own_group
    )[None, None, :]
    cell_scores = (
        jnp.einsum("rqhd,rkhd->rhqk", q4, k4, preferred_element_type=jnp.float32) * score_scale
    )
    cell_scores = jnp.where(allowed[:, None], cell_scores, -1e30)
    tok_scores = (
        jnp.einsum("rqhd,khd->rhqk", q4, sk, preferred_element_type=jnp.float32) * score_scale
    )
    row_top = jnp.maximum(cell_scores.max(-1), tok_scores.max(-1))
    cell_exp = jnp.exp(cell_scores - row_top[..., None])
    tok_exp = jnp.exp(tok_scores - row_top[..., None])
    row_total = cell_exp.sum(-1) + tok_exp.sum(-1)
    mixed = jnp.einsum(
        "rhqk,rkhd->rqhd", cell_exp.astype(jnp.bfloat16), v4, preferred_element_type=jnp.float32
    )
    mixed = mixed + jnp.einsum(
        "rhqk,khd->rqhd", tok_exp.astype(jnp.bfloat16), sv, preferred_element_type=jnp.float32
    )
    attended = mixed / row_total.transpose(0, 2, 1)[..., None]
    attended = attended.reshape(row_count * cols_dev, model_width).astype(jnp.bfloat16)
    all_in = jnp.concatenate([flat_cells, tokens], axis=0)
    all_att = jnp.concatenate([attended, summary_att], axis=0)
    all_out = finish(all_in, all_att, w_out, gain_attn, w_up, w_down, gain_ffn)
    cells_out = all_out[: row_count * cols_dev].reshape(row_count, cols_dev, model_width)
    summary_out = all_out[row_count * cols_dev :]
    return (cells_out, summary_out)


def solution(mesh):
    in_specs = (
        P("band", "col", None),
        P("band", "col", None),
        P("col"),
        P("band", "col"),
        P(),
        P(),
        P(),
        P(),
        P(),
        P(),
    )
    out_specs = (P("band", "col", None), P("col", None))
    return jax.shard_map(local, mesh=mesh, in_specs=in_specs, out_specs=out_specs, check_vma=False)
```

profile of v0, /device:TPU:1, one launch (start us, length us, event | category | flops | bytes accessed | tf_op | source)
XLA Modules:
  0.0 201.5 jit_solution(11720248242947388714)
XLA Ops:
  8.8 0.7 select_bitcast_fusion
  9.5 3.2 %convolution_convert_fusion = bf16[256,2304]{1,0:T(8,128)(2,1)S(1)} fusion(bf16[256,768]{1,0:T(8,128)(2,1)} %bitcast.54, bf16[768,2304]{1,0:T(8,128)(2,1)} %param.14), kind=kOutput, calls=%fused_computation.9 | convolution fusion | flops 906559488 | bytes 5111808 | tf_op jit(solution)/shard_map/dot_general | solution.py:32
  12.8 52.0 %all-reduce.3.cloned.1.call-done = bf16[64,768]{1,0:T(8,128)(2,1)} async-done(((bf16[64,768]{1,0:T(8,128)(2,1)}), bf16[64,768]{1,0:T(8,128)(2,1)}) %all-reduce.3.cloned.1.call-update) | async-done | bytes 98320 | tf_op jit(solution)/shard_map/psum | solution.py:12
  64.8 2.8 %convolution_convert_fusion.2 = bf16[64,2304]{1,0:T(8,128)(2,1)S(1)} fusion(bf16[64,768]{1,0:T(8,128)(2,1)} %all-reduce.3.cloned.1.call-done, bf16[768,2304]{1,0:T(8,128)(2,1)} %param.14), kind=kOutput, calls=%fused_computation.11 | convolution fusion | flops 226639872 | bytes 3932160 | tf_op jit(solution)/shard_map/dot_general | solution.py:32
  67.6 0.7 copy-done.3
  68.3 0.7 fusion.56
  69.0 0.9 reshape.128
  69.9 1.0 convert_multiply_fusion
  70.9 1.6 reshape.127
  72.5 1.3 reduce_sum.93
  73.8 0.6 reduce_sum.92
  74.4 25.6 %pmax.7 = f32[64,12]{1,0:T(8,128)S(1)} all-reduce(f32[64,12]{1,0:T(8,128)S(1)} %multiply_reduce_fusion.3), channel_id=1, replica_groups=mesh['band'=8,'col'=4] {'band'}, use_global_device_ids=true, to_apply=%region_7.8 | all-reduce | flops 768 | bytes 6144 | tf_op jit(solution)/shard_map/pmax | solution.py:67
  100.1 0.6 fusion.45
  100.7 0.6 broadcast_in_dim.21
  101.3 1.4 reshape.129
  102.8 1.3 multiply_reduce_fusion.2
  104.1 0.7 pad_maximum_fusion
  104.9 0.5 all-gather.2.cloned.1.call-update
  105.4 1.0 slice.53
  106.5 0.6 reshape.123
  107.3 0.2 reshape.125
  107.4 0.8 copy.58
  108.2 2.0 %bitcast_reduce_fusion = (f32[4,12,64]{2,0,1:T(4,128)S(1)}, f32[12,64,4,64]{3,1,2,0:T(8,128)}) fusion(bf16[4,64,12,64]{3,2,1,0:T(8,128)(2,1)S(1)} %reshape.123, bf16[64,12,64,1]{2,1,0,3:T(8,128)(2,1)S(1)} %bitcast.53), kind=kOutput, calls=%fused_computation.28 | convolution fusion | flops 25555968 | bytes 1290240 | tf_op jit(solution)/shard_map/rqhd,khd->rhqk/dot_general | solution.py:96
  110.3 49.6 %all-reduce.5.cloned.1.call-done = f32[64,780]{1,0:T(8,128)} async-done(((f32[64,780]{1,0:T(8,128)}), f32[64,780]{1,0:T(8,128)}) %all-reduce.5.cloned.1.call-update) | async-done | bytes 199696 | tf_op jit(solution)/shard_map/psum | solution.py:74
  159.9 0.8 convert_convert_fusion
  160.6 0.2 broadcast_in_dim.23
  161.0 0.2 broadcast_in_dim.22
  161.3 1.0 fusion.41
  162.4 0.8 copy.53
  163.2 4.7 %convolution_convert_fusion.1 = bf16[1024,1536]{1,0:T(8,128)(2,1)S(1)} fusion(bf16[1024,768]{1,0:T(8,128)(2,1)} %bitcast.58, bf16[768,2304]{1,0:T(8,128)(2,1)} %param.14), kind=kOutput, calls=%fused_computation.10 | convolution fusion | flops 2417491968 | bytes 7077888 | tf_op jit(solution)/shard_map/dot_general | solution.py:32
  167.9 1.9 fusion.55
  169.8 2.6 %copy.42 = bf16[4,256,768]{1,2,0:T(8,128)(2,1)} copy(bf16[4,256,768]{2,1,0:T(8,128)(2,1)} %get-tuple-element.3) | data formatting | bytes 3145728 | tf_op jit(solution)/shard_map/slice | solution.py:84
  172.4 2.6 %copy.43 = bf16[4,256,768]{1,2,0:T(8,128)(2,1)} copy(bf16[4,256,768]{2,1,0:T(8,128)(2,1)} %get-tuple-element.2) | data formatting | bytes 3145728 | tf_op jit(solution)/shard_map/slice | solution.py:83
  175.1 2.2 %fusion.8 = (f32[4,12,64]{2,1,0:T(8,128)S(1)}, f32[4,12,64,256]{3,2,1,0:T(8,128)S(1)}) fusion(pred[4,64,256]{2,1,0:T(8,128)(4,1)S(1)} %fusion.39, bf16[4,256,12,64]{1,3,2,0:T(8,128)(2,1)} %bitcast.48, bf16[4,64,12,64]{3,2,1,0:T(8,128)(2,1)S(1)} %reshape.123), kind=kOutput, calls=%fused_computation.14 | convolution fusion | flops 103019520 | bytes 5189632 | tf_op jit(solution)/shard_map/rqhd,rkhd->rhqk/dot_general | solution.py:92
  177.3 1.2 fusion.9
  178.6 1.1 fusion.18
  179.7 0.3 copy-done.1
  180.0 0.4 fusion.27
  180.5 0.4 fusion.21
  180.8 0.6 copy.52
  181.5 1.2 convert_element_type.83
  182.7 1.7 fusion.57
  184.4 0.3 multiply_reduce_fusion.1
  184.7 7.4 %fusion.58 = (f32[320]{0:T(512)S(1)}, f32[320,768]{1,0:T(8,128)S(1)}) fusion(bf16[3072,768]{1,0:T(8,128)(2,1)} %param.18, bf16[768,3072]{1,0:T(8,128)(2,1)} %param.17, f32[320,768]{1,0:T(8,128)S(1)} %get-tuple-element.18, f32[768]{0:T(1024)S(1)} %copy-done.14, f32[320]{0:T(512)S(1)} %add_rsqrt_fusion.1, f32[320]{0:T(512)S(1)} %broadcast_multiply_fusion.1), kind=kOutput, calls=%fused_computation.94 | convolution fusion | flops 3031449344 | bytes 11410176 | tf_op jit(solution)/shard_map/dot_general | solution.py:27
  192.2 0.3 multiply_reduce_fusion
  192.4 0.2 multiply_convert_fusion
  192.6 0.8 slice.62
  193.4 0.6 slice.63
  (49 shorter events, 0.7 us)
Async XLA Ops:
  8.0 174.7 %copy-start = (bf16[768,768]{1,0:T(8,128)(2,1)S(1)}, bf16[768,768]{1,0:T(8,128)(2,1)}, u32[]{:S(2)}) copy-start(bf16[768,768]{1,0:T(8,128)(2,1)} %param.15) | copy-start | bytes 3538948
  8.0 56.8 %all-reduce.3.cloned.1.call-start = ((), (), s32[]{:S(2)}) async-start(), calls=%async_computation | async-start | bytes 196608 | tf_op jit(solution)/shard_map/psum | solution.py:12
  9.5 150.4 %all-reduce.5.cloned.1.call-start = ((), (), s32[]{:S(2)}) async-start(), calls=%async_computation.2 | async-start | bytes 458752 | tf_op jit(solution)/shard_map/psum | solution.py:74
  12.8 57.2 %copy-start.4 = (bf16[256,2304]{1,0:T(8,128)(2,1)}, bf16[256,2304]{1,0:T(8,128)(2,1)S(1)}, u32[]{:S(2)}) copy-start(bf16[256,2304]{1,0:T(8,128)(2,1)S(1)} %convolution_convert_fusion) | copy-start | bytes 3538948
  67.6 0.7 copy-start.3
  100.1 0.6 copy-start.7
  100.7 3.4 %copy-start.11 = (f32[64,12]{1,0:T(8,128)S(1)}, f32[64,12]{1,0:T(8,128)}, u32[]{:S(2)}) copy-start(f32[64,12]{1,0:T(8,128)} %get-tuple-element.10) | copy-start | bytes 9220
  101.3 5.8 %copy-start.13 = (s32[4,64]{1,0:T(4,128)S(1)}, s32[4,64]{1,0:T(4,128)}, u32[]{:S(2)}) copy-start(s32[4,64]{1,0:T(4,128)} %param.13) | copy-start | bytes 3076
  101.3 5.9 %copy-start.6 = (bf16[64,768]{1,0:T(8,128)(2,1)S(1)}, bf16[64,768]{1,0:T(8,128)(2,1)}, u32[]{:S(2)}) copy-start(bf16[64,768]{1,0:T(8,128)(2,1)} %get-tuple-element.8) | copy-start | bytes 294916
  104.8 55.0 %copy-start.8 = (f32[64,12]{1,0:T(8,128)S(1)}, f32[64,12]{1,0:T(8,128)}, u32[]{:S(2)}) copy-start(f32[64,12]{1,0:T(8,128)} %copy-done.7) | copy-start | bytes 9220
  104.9 58.3 %all-gather.2.cloned.1.call-start = ((), (), s32[]{:S(2)}) async-start(), calls=%async_computation.1 | async-start | bytes 1966080 | tf_op jit(solution)/shard_map/all_gather | solution.py:54
  175.1 3.5 %copy-start.2 = (bf16[4,256,768]{1,2,0:T(8,128)(2,1)S(1)}, bf16[4,256,768]{1,2,0:T(8,128)(2,1)}, u32[]{:S(2)}) copy-start(bf16[4,256,768]{1,2,0:T(8,128)(2,1)} %copy.42) | copy-start | bytes 4718596
  178.6 1.4 copy-start.1
  178.6 1.8 copy-start.9
  180.4 2.3 %copy-start.5 = (bf16[4,64,768]{2,1,0:T(8,128)(2,1)S(1)}, bf16[4,64,768]{2,1,0:T(8,128)(2,1)}, u32[]{:S(2)}) copy-start(bf16[4,64,768]{2,1,0:T(8,128)(2,1)} %param.10) | copy-start | bytes 1179652
  180.5 2.2 %copy-start.10 = (bf16[64,768]{0,1:T(8,128)(2,1)S(1)}, bf16[64,768]{0,1:T(8,128)(2,1)}, u32[]{:S(2)}) copy-start(bf16[64,768]{0,1:T(8,128)(2,1)} %copy.53) | copy-start | bytes 294916
  182.7 2.0 copy-start.14
  184.7 7.7 %copy-start.12 = (f32[768]{0:T(1024)S(1)}, f32[768]{0:T(1024)}, u32[]{:S(2)}) copy-start(f32[768]{0:T(1024)} %param.19) | copy-start | bytes 9220
Sparse Core Ops, SparseCore 0:
  11.7 53.0 all-reduce.2
  105.0 54.8 all-reduce.4
Sparse Core Ops, SparseCore 1:
  107.2 32.3 all-gather.1
where the time goes:
time: 202 us; the launch traced here: 201 us
  waiting for transfers between devices  102 us (50%)
  matrix products  25.7 us (13%)
  blocking collectives  25.6 us (13%)
  local copies, waits for them, and re-layouts  20.1 us (10%)
  between operations  16.6 us (8%)
  other arithmetic  11.3 us (6%)
    psum x1, waiting for transfers between devices, spread_2(): return lax.psum(kept, axis)  52 us
    psum x1, waiting for transfers between devices, local(): packed = lax.psum(packed, 'band')  49.6 us
    pmax x1, blocking collectives, local(): col_top = jnp.maximum(lax.pmax(col_scores.max(0), 'band'), self_scores)  25.6 us
    dot_general x3, matrix products, project(): jnp.dot(values, weight, preferred_element_type=jnp.float32)  10.8 us
    dot_general x1, matrix products, finish(): outer_out = jnp.dot(inner_act, w_down, preferred_element_type=jnp.float32)  7.43 us
    slice x2, local copies, waits for them, and re-layouts, local(): row_kv[:, :, :model_width].reshape(row_count, width_now, HEADS, HEAD_DIM)  4.55 us
  transfers between devices with their start and end apart: 3, of which 2 were waited for; matrix products, arithmetic and copies ran while one was open for 6% of the time, Pallas kernels for 0%

commit v1 on v0

--- a/solution.py
+++ b/solution.py
@@ -9,7 +9,7 @@
 
 def spread_2(value, axis, source):
     kept = jnp.where(lax.axis_index(axis) == source, value, 0).astype(value.dtype)
-    return lax.psum(kept, axis)
+    return jnp.sum(lax.all_gather(kept, axis), axis=0)
 
 
 def layer_norm(values, gain_vec):

time: 202 us -> 167 us (0.83)
  waiting for transfers between devices: 102 us -> 50.2 us
  blocking collectives: 25.6 us -> 42.4 us
    psum x1 -> x0, waiting for transfers between devices: 52 us -> none  [spread_2(): return lax.psum(kept, axis)]
    all_gather x0 -> x1, blocking collectives: none -> 17.5 us  [spread_2(): return jnp.sum(lax.all_gather(kept, axis), axis=0)]
  transfers between devices with their start and end apart: 3 -> 2, of which waited for: 2 -> 1; matrix products, arithmetic and copies ran while one was open for 6% -> 5% of each run, Pallas kernels for 0% -> 0%
where the time goes in v1:
time: 167 us
  waiting for transfers between devices  50.2 us (30%)
  blocking collectives  42.4 us (25%)
  matrix products  25.6 us (15%)
  local copies, waits for them, and re-layouts  21.1 us (13%)
  between operations  16.6 us (10%)
  other arithmetic  10.7 us (6%)
    psum x1, waiting for transfers between devices, local(): packed = lax.psum(packed, 'band')  49.6 us
    pmax x1, blocking collectives, local(): col_top = jnp.maximum(lax.pmax(col_scores.max(0), 'band'), self_scores)  24.9 us
    all_gather x1, blocking collectives, spread_2(): return jnp.sum(lax.all_gather(kept, axis), axis=0)  17.5 us
    dot_general x3, matrix products, project(): jnp.dot(values, weight, preferred_element_type=jnp.float32)  10.6 us
    dot_general x1, matrix products, finish(): outer_out = jnp.dot(inner_act, w_down, preferred_element_type=jnp.float32)  7.43 us
    slice x2, local copies, waits for them, and re-layouts, local(): row_kv[:, :, :model_width].reshape(row_count, width_now, HEADS, HEAD_DIM)  4.55 us
  transfers between devices with their start and end apart: 2, of which 1 were waited for; matrix products, arithmetic and copies ran while one was open for 5% of the time, Pallas kernels for 0%

profile of v1, /device:TPU:1, one launch (start us, length us, event | category | flops | bytes accessed | tf_op | source)
XLA Modules:
  0.0 166.7 jit_solution(7154143325895878319)
XLA Ops:
  8.8 17.5 %all_gather.7 = bf16[8,64,768]{2,1,0:T(8,128)(2,1)S(1)} all-gather(bf16[1,64,768]{2,1,0:T(8,128)(2,1)S(1)} %broadcast_select_fusion), channel_id=1, replica_groups=mesh['band'=8,'col'=4] {'band'}, dimensions={0}, use_global_device_ids=true | all-gather | bytes 884736 | tf_op jit(solution)/shard_map/all_gather | solution.py:12
  26.4 2.8 %convolution_convert_fusion.2 = bf16[64,2304]{1,0:T(8,128)(2,1)S(1)} fusion(bf16[64,768]{1,0:T(8,128)(2,1)S(1)} %reduce_sum.102, bf16[768,2304]{1,0:T(8,128)(2,1)} %param.14), kind=kOutput, calls=%fused_computation.11 | convolution fusion | flops 226639872 | bytes 3932160 | tf_op jit(solution)/shard_map/dot_general | solution.py:32
  29.3 0.7 copy-done.3
  29.9 0.7 fusion.56
  30.6 0.9 reshape.125
  31.6 3.1 %convolution_convert_fusion = bf16[256,2304]{1,0:T(8,128)(2,1)S(1)} fusion(bf16[256,768]{1,0:T(8,128)(2,1)S(1)} %bitcast.52, bf16[768,2304]{1,0:T(8,128)(2,1)} %param.14), kind=kOutput, calls=%fused_computation.9 | convolution fusion | flops 906559488 | bytes 5111808 | tf_op jit(solution)/shard_map/dot_general | solution.py:32
  34.7 1.0 copy-done.4
  35.7 1.0 convert_multiply_fusion
  36.7 1.6 reshape.124
  38.3 1.3 reduce_sum.106
  39.5 0.6 reduce_sum.105
  40.2 24.9 %pmax.7 = f32[64,12]{1,0:T(8,128)S(1)} all-reduce(f32[64,12]{1,0:T(8,128)S(1)} %multiply_reduce_fusion.3), channel_id=1, replica_groups=mesh['band'=8,'col'=4] {'band'}, use_global_device_ids=true, to_apply=%region_7.8 | all-reduce | flops 768 | bytes 6144 | tf_op jit(solution)/shard_map/pmax | solution.py:67
  65.1 0.6 fusion.45
  65.7 0.6 broadcast_in_dim.21
  66.4 1.4 reshape.126
  67.8 1.3 multiply_reduce_fusion.2
  69.1 0.7 pad_maximum_fusion
  69.9 0.5 all-gather.2.cloned.1.call-update
  70.5 1.0 slice.53
  71.5 0.6 reshape.120
  72.1 0.2 reshape.122
  72.3 0.8 copy.58
  73.3 2.0 %bitcast_reduce_fusion = (f32[4,12,64]{2,0,1:T(4,128)S(1)}, f32[12,64,4,64]{3,1,2,0:T(8,128)}) fusion(bf16[4,64,12,64]{3,2,1,0:T(8,128)(2,1)S(1)} %reshape.120, bf16[64,12,64,1]{2,1,0,3:T(8,128)(2,1)S(1)} %bitcast.51), kind=kOutput, calls=%fused_computation.28 | convolution fusion | flops 25555968 | bytes 1290240 | tf_op jit(solution)/shard_map/rqhd,khd->rhqk/dot_general | solution.py:96
  75.3 49.6 %all-reduce.2.cloned.1.call-done = f32[64,780]{1,0:T(8,128)} async-done(((f32[64,780]{1,0:T(8,128)}), f32[64,780]{1,0:T(8,128)}) %all-reduce.2.cloned.1.call-update) | async-done | bytes 199696 | tf_op jit(solution)/shard_map/psum | solution.py:74
  125.0 0.8 convert_convert_fusion
  125.7 0.2 broadcast_in_dim.23
  126.1 0.2 broadcast_in_dim.22
  126.4 1.0 fusion.41
  127.4 0.8 copy.53
  128.3 4.7 %convolution_convert_fusion.1 = bf16[1024,1536]{1,0:T(8,128)(2,1)S(1)} fusion(bf16[1024,768]{1,0:T(8,128)(2,1)} %bitcast.56, bf16[768,2304]{1,0:T(8,128)(2,1)} %param.14), kind=kOutput, calls=%fused_computation.10 | convolution fusion | flops 2417491968 | bytes 7077888 | tf_op jit(solution)/shard_map/dot_general | solution.py:32
  133.0 1.9 %fusion.55 = (bf16[4,256,768]{2,1,0:T(8,128)(2,1)}, bf16[4,256,768]{2,1,0:T(8,128)(2,1)}) fusion(bf16[4,256,1536]{2,1,0:T(8,128)(2,1)S(1)} %bitcast.47), kind=kLoop, calls=%fused_computation.91 | loop fusion | bytes 6291456 | tf_op jit(solution)/shard_map/slice | solution.py:83
  134.9 2.6 %copy.42 = bf16[4,256,768]{1,2,0:T(8,128)(2,1)} copy(bf16[4,256,768]{2,1,0:T(8,128)(2,1)} %get-tuple-element.3) | data formatting | bytes 3145728 | tf_op jit(solution)/shard_map/slice | solution.py:84
  137.5 2.6 %copy.43 = bf16[4,256,768]{1,2,0:T(8,128)(2,1)} copy(bf16[4,256,768]{2,1,0:T(8,128)(2,1)} %get-tuple-element.2) | data formatting | bytes 3145728 | tf_op jit(solution)/shard_map/slice | solution.py:83
  140.1 2.3 %fusion.8 = (f32[4,12,64]{2,1,0:T(8,128)S(1)}, f32[4,12,64,256]{3,2,1,0:T(8,128)S(1)}) fusion(pred[4,64,256]{2,1,0:T(8,128)(4,1)S(1)} %fusion.39, bf16[4,256,12,64]{1,3,2,0:T(8,128)(2,1)} %bitcast.46, bf16[4,64,12,64]{3,2,1,0:T(8,128)(2,1)S(1)} %reshape.120), kind=kOutput, calls=%fused_computation.14 | convolution fusion | flops 103019520 | bytes 5189632 | tf_op jit(solution)/shard_map/rqhd,rkhd->rhqk/dot_general | solution.py:92
  142.4 1.2 fusion.9
  143.7 1.1 fusion.18
  144.8 0.3 copy-done.1
  145.1 0.4 fusion.27
  145.6 0.4 fusion.21
  145.9 0.6 copy.52
  146.6 1.2 convert_element_type.85
  147.8 1.8 %fusion.57 = (f32[320]{0:T(512)S(1)}, f32[320,768]{1,0:T(8,128)S(1)}) fusion(bf16[768,768]{1,0:T(8,128)(2,1)S(1)} %copy-done, bf16[64,768]{0,1:T(8,128)(2,1)} %copy.53, bf16[256,768]{0,1:T(8,128)(2,1)} %convert_element_type.85, bf16[64,768]{1,0:T(8,128)(2,1)S(1)} %copy-done.9, bf16[256,768]{1,0:T(8,128)(2,1)S(1)} %bitcast.53), kind=kOutput, calls=%fused_computation.93 | convolution fusion | flops 379944640 | bytes 3147008 | tf_op jit(solution)/shard_map/dot_general | solution.py:22
  149.6 0.3 multiply_reduce_fusion.1
  149.9 7.4 %fusion.58 = (f32[320]{0:T(512)S(1)}, f32[320,768]{1,0:T(8,128)S(1)}) fusion(bf16[3072,768]{1,0:T(8,128)(2,1)} %param.18, bf16[768,3072]{1,0:T(8,128)(2,1)} %param.17, f32[320,768]{1,0:T(8,128)S(1)} %get-tuple-element.18, f32[768]{0:T(1024)S(1)} %copy-done.16, f32[320]{0:T(512)S(1)} %add_rsqrt_fusion.1, f32[320]{0:T(512)S(1)} %broadcast_multiply_fusion.1), kind=kOutput, calls=%fused_computation.94 | convolution fusion | flops 3031449344 | bytes 11410176 | tf_op jit(solution)/shard_map/dot_general | solution.py:27
  157.3 0.3 multiply_reduce_fusion
  157.6 0.2 multiply_convert_fusion
  157.8 0.8 slice.62
  158.6 0.6 slice.63
  (52 shorter events, 0.8 us)
Async XLA Ops:
  8.0 139.8 %copy-start = (bf16[768,768]{1,0:T(8,128)(2,1)S(1)}, bf16[768,768]{1,0:T(8,128)(2,1)}, u32[]{:S(2)}) copy-start(bf16[768,768]{1,0:T(8,128)(2,1)} %param.15) | copy-start | bytes 3538948
  8.0 116.9 %all-reduce.2.cloned.1.call-start = ((), (), s32[]{:S(2)}) async-start(), calls=%async_computation.1 | async-start | bytes 458752 | tf_op jit(solution)/shard_map/psum | solution.py:74
  26.3 5.2 %copy-start.5 = (bf16[4,64,768]{2,1,0:T(8,128)(2,1)S(1)}, bf16[4,64,768]{2,1,0:T(8,128)(2,1)}, u32[]{:S(2)}) copy-start(bf16[4,64,768]{2,1,0:T(8,128)(2,1)} %param.10) | copy-start | bytes 1179652
  26.4 8.2 %copy-start.8 = (bf16[64,768]{1,0:T(8,128)(2,1)}, bf16[64,768]{1,0:T(8,128)(2,1)S(1)}, u32[]{:S(2)}) copy-start(bf16[64,768]{1,0:T(8,128)(2,1)S(1)} %reduce_sum.102) | copy-start | bytes 294916
  29.2 0.7 copy-start.3
  34.7 1.0 copy-start.4
  65.1 0.6 copy-start.10
  65.7 3.4 %copy-start.13 = (f32[64,12]{1,0:T(8,128)S(1)}, f32[64,12]{1,0:T(8,128)}, u32[]{:S(2)}) copy-start(f32[64,12]{1,0:T(8,128)} %get-tuple-element.10) | copy-start | bytes 9220
  66.4 5.8 %copy-start.7 = (bf16[64,768]{1,0:T(8,128)(2,1)S(1)}, bf16[64,768]{1,0:T(8,128)(2,1)}, u32[]{:S(2)}) copy-start(bf16[64,768]{1,0:T(8,128)(2,1)} %get-tuple-element.8) | copy-start | bytes 294916
  67.8 5.3 %copy-start.15 = (s32[4,64]{1,0:T(4,128)S(1)}, s32[4,64]{1,0:T(4,128)}, u32[]{:S(2)}) copy-start(s32[4,64]{1,0:T(4,128)} %param.13) | copy-start | bytes 3076
  69.9 55.1 %copy-start.11 = (f32[64,12]{1,0:T(8,128)S(1)}, f32[64,12]{1,0:T(8,128)}, u32[]{:S(2)}) copy-start(f32[64,12]{1,0:T(8,128)} %copy-done.10) | copy-start | bytes 9220
  69.9 58.4 %all-gather.2.cloned.1.call-start = ((), (), s32[]{:S(2)}) async-start(), calls=%async_computation | async-start | bytes 1966080 | tf_op jit(solution)/shard_map/all_gather | solution.py:54
  140.1 3.5 %copy-start.2 = (bf16[4,256,768]{1,2,0:T(8,128)(2,1)S(1)}, bf16[4,256,768]{1,2,0:T(8,128)(2,1)}, u32[]{:S(2)}) copy-start(bf16[4,256,768]{1,2,0:T(8,128)(2,1)} %copy.42) | copy-start | bytes 4718596
  143.7 1.4 copy-start.1
  143.7 1.8 %copy-start.12 = (bf16[64,768]{0,1:T(8,128)(2,1)S(1)}, bf16[64,768]{0,1:T(8,128)(2,1)}, u32[]{:S(2)}) copy-start(bf16[64,768]{0,1:T(8,128)(2,1)} %copy.58) | copy-start | bytes 294916
  145.5 2.3 %copy-start.6 = (bf16[4,64,768]{2,1,0:T(8,128)(2,1)S(1)}, bf16[4,64,768]{2,1,0:T(8,128)(2,1)}, u32[]{:S(2)}) copy-start(bf16[4,64,768]{2,1,0:T(8,128)(2,1)} %param.10) | copy-start | bytes 1179652
  145.6 2.2 %copy-start.9 = (bf16[64,768]{1,0:T(8,128)(2,1)S(1)}, bf16[64,768]{1,0:T(8,128)(2,1)}, u32[]{:S(2)}) copy-start(bf16[64,768]{1,0:T(8,128)(2,1)} %copy-done.8) | copy-start | bytes 294916
  147.8 2.1 %copy-start.16 = (f32[768]{0:T(1024)S(1)}, f32[768]{0:T(1024)}, u32[]{:S(2)}) copy-start(f32[768]{0:T(1024)} %param.16) | copy-start | bytes 9220
  149.9 7.7 %copy-start.14 = (f32[768]{0:T(1024)S(1)}, f32[768]{0:T(1024)}, u32[]{:S(2)}) copy-start(f32[768]{0:T(1024)} %param.19) | copy-start | bytes 9220
Sparse Core Ops, SparseCore 0:
  70.0 54.8 all-reduce.1
Sparse Core Ops, SparseCore 1:
  72.4 32.3 all-gather.1
